TPU v7x, 32 devices: a whole 2x2x4 slice. The times are simulated.
32 devices in a mesh: ctx: 8 (over y, x, core), tp: 4 (over z).
Axes of the slice: x: 2, y: 2, z: 4, core: 2. Of those that a mesh axis runs over, the one named last changes fastest.
Arguments:
- tokens: bfloat16 [4096, 4096], P(('ctx', 'tp')), may hold values from -6 to 6
- spike_query: int32 [4096, 32], P('ctx', 'tp'), may hold values 0 or 1
- spike_key: int32 [4096, 32], P('ctx', 'tp'), may hold values 0 or 1
- qkv_weight: bfloat16 [4096, 3, 4096], P(None, None, 'tp'), may hold values from -0.09375 to 0.09375
- qkv_blocks: int32 [3, 32, 32], P(None, None, 'tp'), may hold values 0 or 1
- out_weight: bfloat16 [4096, 4096], P('tp'), may hold values from -0.09375 to 0.09375
- out_blocks: int32 [32, 32], P('tp'), may hold values 0 or 1
- cotangent: bfloat16 [4096, 4096], P(('ctx', 'tp')), may hold values from -6 to 6
Outputs:
- layer_out: bfloat16 [4096, 4096], P(('ctx', 'tp'))
- token_grad: bfloat16 [4096, 4096], P(('ctx', 'tp'))
- qkv_grad: float32 [4096, 3, 4096], P('ctx', None, 'tp')
- out_grad: float32 [4096, 4096], P('tp', 'ctx')
All inputs are finite; a program needn't handle non-finite values. No bound on the sum of `spike_query` or of `spike_key` or of `qkv_blocks` or of `out_blocks` on one device may be relied on, other than what follows from the above.
Results may differ from a plain program's by a relative error of at most 0.014.
Values may be sent and summed in bfloat16 or wider, within the bound.
No kernel may reach another device: no remote copies, remote signals or barrier semaphores. Data moves between devices by JAX's collectives and lax.ppermute only.
A program may use at most 320 MiB of HBM per device.

v0:
```python
import math
import jax
import jax.numpy as jnp
from jax import lax
from jax.sharding import PartitionSpec as P

BLOCK = 128
EPSILON = 1e-05


def carried_in(value, axis, join, neutral):
    place = lax.axis_index(axis)
    gathered = lax.all_gather(value.astype(jnp.bfloat16), axis)
    state = jnp.zeros_like(value) + jnp.asarray(neutral, value.dtype)

    def carried_one(lap, state):
        return join(state, lax.dynamic_index_in_dim(gathered, lap, 0, False).astype(value.dtype))

    return lax.fori_loop(0, place, carried_one, state)


def entering(value, axis, join, neutral):
    count = lax.axis_size(axis)
    place = lax.axis_index(axis)
    ahead = count - 1 - place
    gathered = lax.all_gather(
        value.astype(jnp.bfloat16 if value.dtype == jnp.float32 else value.dtype), axis
    )
    state = jnp.zeros_like(value) + jnp.asarray(neutral, value.dtype)

    def entering_one(lap, state):
        source = count - 1 - lap
        return join(state, lax.dynamic_index_in_dim(gathered, source, 0, False).astype(value.dtype))

    return lax.fori_loop(0, ahead, entering_one, state)


def expand_blocks(blocks):
    row_blocks, col_blocks = blocks.shape
    spread = jnp.broadcast_to(
        blocks.astype(jnp.bfloat16)[:, None, :, None], (row_blocks, BLOCK, col_blocks, BLOCK)
    )
    return spread.reshape(row_blocks * BLOCK, col_blocks * BLOCK)


def qkv_keep_table(qkv_blocks):
    tables = [expand_blocks(qkv_blocks[projection]) for projection in range(3)]
    return jnp.stack(tables, axis=1)


def add_states(earlier, following):
    return earlier + following


def on_device(
    tokens, spike_query, spike_key, qkv_weight, qkv_blocks, out_weight, out_blocks, cotangent
):
    model_width = tokens.shape[1]
    block_rows = spike_query.shape[0]
    local_heads = spike_query.shape[1]
    features = qkv_weight.shape[2]
    head_width = features // local_heads
    highest = lax.Precision.HIGHEST
    qkv_keep = qkv_keep_table(qkv_blocks).reshape(model_width, 3 * features)
    qkv_used = qkv_weight.reshape(model_width, 3 * features) * qkv_keep
    out_used = out_weight * expand_blocks(out_blocks)
    gathered = lax.all_gather(tokens, "tp", axis=0, tiled=True)
    projected = jnp.dot(gathered, qkv_used, preferred_element_type=jnp.float32).astype(jnp.bfloat16)
    projected = projected.reshape(block_rows, 3, local_heads, head_width)
    query_spikes = spike_query.astype(jnp.bfloat16)[:, :, None]
    key_spikes = spike_key.astype(jnp.bfloat16)[:, :, None]
    query_spiked = projected[:, 0] * query_spikes
    key_spiked = projected[:, 1] * key_spikes
    values = projected[:, 2]
    query_wide = query_spiked.astype(jnp.float32)
    key_wide = key_spiked.astype(jnp.float32)
    local_state = jnp.einsum("shd,she->hde", key_spiked, values, preferred_element_type=jnp.float32)
    zeros_state = jnp.zeros_like(local_state)
    prior_state = carried_in(local_state, "ctx", add_states, zeros_state)
    positions = lax.iota(jnp.int32, block_rows)
    causal_keep = positions[:, None] >= positions[None, :]
    scores = jnp.einsum(
        "thd,shd->hts", query_spiked, key_spiked, preferred_element_type=jnp.float32
    )
    scores = jnp.where(causal_keep, scores, 0.0).astype(jnp.bfloat16)
    mixed_rows = jnp.einsum("hts,she->the", scores, values, preferred_element_type=jnp.float32)
    mixed_rows = mixed_rows + jnp.einsum("thd,hde->the", query_wide, prior_state, precision=highest)
    inv_rms = lax.rsqrt(jnp.mean(mixed_rows * mixed_rows, axis=-1, keepdims=True) + EPSILON)
    normed = mixed_rows * inv_rms
    attended = normed.astype(jnp.bfloat16).reshape(block_rows, features)
    row_piece = attended
    head_sum = lax.psum_scatter(
        jnp.dot(row_piece, out_used, preferred_element_type=jnp.float32).astype(jnp.bfloat16),
        "tp",
        scatter_dimension=0,
        tiled=True,
    ).astype(jnp.float32)
    layer_out = (tokens.astype(jnp.float32) + head_sum).astype(jnp.bfloat16)
    grad_rows = lax.all_gather(cotangent, "tp", axis=0, tiled=True)
    grad_attended = jnp.einsum("tm,fm->tf", grad_rows, out_used, preferred_element_type=jnp.float32)
    grad_attended = grad_attended.reshape(block_rows, local_heads, head_width)
    inner_mean = jnp.mean(grad_attended * normed, axis=-1, keepdims=True)
    grad_mixed = inv_rms * (grad_attended - normed * inner_mean)
    grad_low = grad_mixed.astype(jnp.bfloat16)
    local_adjoint = jnp.einsum("thd,the->hde", query_wide, grad_mixed, precision=highest)
    after_state = entering(local_adjoint, "ctx", add_states, zeros_state)
    adjoint_scores = jnp.einsum(
        "the,she->hts", grad_low, values, preferred_element_type=jnp.float32
    )
    adjoint_scores = jnp.where(causal_keep, adjoint_scores, 0.0).astype(jnp.bfloat16)
    grad_query = jnp.einsum(
        "hts,shd->thd", adjoint_scores, key_spiked, preferred_element_type=jnp.float32
    )
    grad_query = grad_query + jnp.einsum("the,hde->thd", grad_mixed, prior_state, precision=highest)
    grad_key = jnp.einsum(
        "hts,thd->shd", adjoint_scores, query_spiked, preferred_element_type=jnp.float32
    )
    grad_key = grad_key + jnp.einsum(
        "she,hde->shd", values.astype(jnp.float32), after_state, precision=highest
    )
    grad_value = jnp.einsum("hts,the->she", scores, grad_low, preferred_element_type=jnp.float32)
    grad_value = grad_value + jnp.einsum("shd,hde->she", key_wide, after_state, precision=highest)
    grad_proj = jnp.stack(
        [
            (grad_query * query_spikes.astype(jnp.float32)).astype(jnp.bfloat16),
            (grad_key * key_spikes.astype(jnp.float32)).astype(jnp.bfloat16),
            grad_value.astype(jnp.bfloat16),
        ],
        axis=1,
    ).reshape(block_rows, 3 * features)
    row_piece = grad_proj
    token_sum = lax.psum_scatter(
        jnp.einsum("tc,mc->tm", row_piece, qkv_used, preferred_element_type=jnp.float32).astype(
            jnp.bfloat16
        ),
        "tp",
        scatter_dimension=0,
        tiled=True,
    ).astype(jnp.float32)
    token_grad = (cotangent.astype(jnp.float32) + token_sum).astype(jnp.bfloat16)
    out_keep_cols = expand_blocks(jnp.transpose(out_blocks))
    slice_rows = model_width // lax.axis_size("ctx")
    norm_factor = 1.0 / math.sqrt(block_rows * lax.axis_size("ctx"))
    qkv_part = jnp.einsum("tm,tc->mc", gathered, grad_proj, preferred_element_type=jnp.float32)
    qkv_part = qkv_part * qkv_keep
    out_part = jnp.einsum("tm,tf->mf", grad_rows, attended, preferred_element_type=jnp.float32)
    out_part = out_part * out_keep_cols
    weight_sum = lax.psum_scatter(
        jnp.concatenate([qkv_part, out_part], axis=1).astype(jnp.bfloat16),
        "ctx",
        scatter_dimension=0,
        tiled=True,
    ).astype(jnp.float32)
    weight_sum = weight_sum * norm_factor
    qkv_grad = weight_sum[:, : 3 * features].reshape(slice_rows, 3, features)
    out_grad = jnp.transpose(weight_sum[:, 3 * features :])
    return (layer_out, token_grad, qkv_grad, out_grad)


def solution(mesh):
    placed = (
        P(("ctx", "tp"), None),
        P("ctx", "tp"),
        P("ctx", "tp"),
        P(None, None, "tp"),
        P(None, None, "tp"),
        P("tp", None),
        P("tp", None),
        P(("ctx", "tp"), None),
    )
    return jax.shard_map(
        on_device,
        mesh=mesh,
        in_specs=placed,
        out_specs=(
            P(("ctx", "tp"), None),
            P(("ctx", "tp"), None),
            P("ctx", None, "tp"),
            P("tp", "ctx"),
        ),
        check_vma=False,
    )
```

profile of v0, /device:TPU:0, one launch (start us, length us, event | category | flops | bytes accessed | tf_op | source)
XLA Modules:
  0.0 714.5 jit_solution(4649358727200529671)
XLA Ops:
  8.0 32.2 %copy.43 = bf16[4096,3,1024]{0,2,1:T(8,128)(2,1)} copy(bf16[4096,3,1024]{2,0,1:T(8,128)(2,1)} %param.15) | data formatting | bytes 50331648 | tf_op args[3]
  40.2 4.5 broadcast_in_dim.22
  44.7 13.3 %stack_reshape.9 = bf16[4096,1,1024]{0,2,1:T(8,128)(2,1)} reshape(bf16[32,128,8,128]{1,0,3,2:T(8,128)(2,1)} %broadcast_in_dim.22) | data formatting | bytes 16777216 | tf_op jit(solution)/shard_map/stack;reshape | solution.py:48
  58.0 4.5 broadcast_in_dim.25
  62.5 13.3 %stack_reshape.10 = bf16[4096,1,1024]{0,2,1:T(8,128)(2,1)} reshape(bf16[32,128,8,128]{1,0,3,2:T(8,128)(2,1)} %broadcast_in_dim.25) | data formatting | bytes 16777216 | tf_op jit(solution)/shard_map/stack;reshape | solution.py:48
  75.8 4.5 broadcast_in_dim.26
  80.3 13.4 %stack_reshape.11 = bf16[4096,1,1024]{0,2,1:T(8,128)(2,1)} reshape(bf16[32,128,8,128]{1,0,3,2:T(8,128)(2,1)} %broadcast_in_dim.26) | data formatting | bytes 16777216 | tf_op jit(solution)/shard_map/stack;reshape | solution.py:48
  93.7 7.8 %constant_dynamic-update-slice_fusion.2 = bf16[4096,3,1024]{0,2,1:T(8,128)(2,1)} fusion(bf16[4096,1,1024]{0,2,1:T(8,128)(2,1)} %stack_reshape.9), kind=kLoop, calls=%fused_computation.51 | loop fusion | bytes 16777216
  101.5 7.7 %constant_dynamic-update-slice_fusion.1 = bf16[4096,3,1024]{0,2,1:T(8,128)(2,1)} fusion(bf16[4096,3,1024]{0,2,1:T(8,128)(2,1)} %constant_dynamic-update-slice_fusion.2, bf16[4096,1,1024]{0,2,1:T(8,128)(2,1)} %stack_reshape.10), kind=kLoop, calls=%fused_computation.50 | loop fusion | bytes 16777216
  109.2 7.8 %constant_dynamic-update-slice_fusion = bf16[4096,3,1024]{0,2,1:T(8,128)(2,1)} fusion(bf16[4096,3,1024]{0,2,1:T(8,128)(2,1)} %constant_dynamic-update-slice_fusion.1, bf16[4096,1,1024]{0,2,1:T(8,128)(2,1)} %stack_reshape.11), kind=kLoop, calls=%fused_computation.49 | loop fusion | bytes 16777216 | tf_op jit(solution)/shard_map/stack | solution.py:48
  117.0 28.6 %mul.82 = bf16[4096,3,1024]{0,2,1:T(8,128)(2,1)} multiply(bf16[4096,3,1024]{0,2,1:T(8,128)(2,1)} %copy.43, bf16[4096,3,1024]{0,2,1:T(8,128)(2,1)} %constant_dynamic-update-slice_fusion) | non-fusion elementwise | flops 12582912 | bytes 75497472 | tf_op jit(solution)/shard_map/mul | solution.py:65
  145.7 18.2 %convolution_convert_fusion.2 = bf16[3072,512]{1,0:T(8,128)(2,1)S(1)} fusion(bf16[4096,3072]{0,1:T(8,128)(2,1)} %bitcast.148, bf16[512,4096]{1,0:T(8,128)(2,1)} %all-gather.7.cloned.1.call-done), kind=kOutput, calls=%fused_computation.13 | convolution fusion | flops 12886474752 | bytes 32505856 | tf_op jit(solution)/shard_map/dot_general | solution.py:68
  163.9 1.5 convolution_convert_fusion.3
  166.5 1.4 select_convert_fusion.1
  167.9 2.0 copy-done.4
  169.9 2.8 fusion.12
  172.7 22.8 %all-gather.11.cloned.1.call-done = bf16[64,128,128]{2,1,0:T(8,128)(2,1)} async-done(((bf16[8,128,128]{2,1,0:T(8,128)(2,1)}), bf16[64,128,128]{2,1,0:T(8,128)(2,1)}) %all-gather.11.cloned.1.call-update) | async-done | bytes 2097168 | tf_op jit(solution)/shard_map/all_gather | solution.py:13
  195.5 3.1 fusion.5
  198.6 79.2 %all-gather.9.cloned.1.call-done = bf16[512,4096]{1,0:T(8,128)(2,1)} async-done(((bf16[128,4096]{1,0:T(8,128)(2,1)}), bf16[512,4096]{1,0:T(8,128)(2,1)}) %all-gather.9.cloned.1.call-update) | async-done | bytes 4194320 | tf_op jit(solution)/shard_map/all_gather | solution.py:99
  277.8 1.1 broadcast_in_dim.30
  279.0 12.4 %multiply_reduce_fusion = (f32[512,8]{0,1:T(8,128)S(1)}, f32[1024,512]{1,0:T(8,128)S(1)}) fusion(f32[8,128,512]{2,1,0:T(8,128)S(1)} %get-tuple-element.125, f32[512,8]{0,1:T(8,128)S(1)} %add_rsqrt_fusion, bf16[512,4096]{1,0:T(8,128)(2,1)} %all-gather.9.cloned.1.call-done, bf16[1024,4096]{1,0:T(8,128)(2,1)} %param.17, bf16[128,8,32,128]{3,2,1,0:T(8,128)(2,1)S(1)} %bitcast.145), kind=kOutput, calls=%fused_computation.27 | convolution fusion | flops 4300730368 | bytes 25198592 | tf_op jit(solution)/shard_map/tm,fm->tf/dot_general | solution.py:100
  291.4 3.2 subtract_multiply_fusion
  294.6 3.1 convolution_convert_fusion.4
  298.0 13.5 %convolution_convert_fusion.1 = bf16[512,4096]{1,0:T(8,128)(2,1)} fusion(bf16[512,1024]{0,1:T(8,128)(2,1)} %bitcast.160, bf16[1024,4096]{1,0:T(8,128)(2,1)} %param.17, bf16[128,8,32,128]{3,2,1,0:T(8,128)(2,1)} %bitcast.146), kind=kOutput, calls=%fused_computation.12 | convolution fusion | flops 4301258752 | bytes 22020096 | tf_op jit(solution)/shard_map/dot_general | solution.py:93
  311.5 2.7 select_convert_fusion
  314.3 1.5 fusion.22
  315.8 2.9 fusion.8
  318.6 2.1 fusion.17
  321.6 2.1 fusion.13
  324.3 8.2 %while.23 = (s32[]{:T(128)}, f32[8,128,128]{2,1,0:T(8,128)S(1)}, s32[]{:T(128)}, bf16[8,8,128,128]{3,2,1,0:T(8,128)(2,1)}, s32[]{:T(128)}, /*index=5*/s32[]{:T(128)}, s32[]{:T(128)}, s32[]{:T(128)}) while((s32[]{:T(128)}, f32[8,128,128]{2,1,0:T(8,128)S(1)}, s32[]{:T(128)}, bf16[8,8,128,128]{3,2,1,0:T(8,128)(2,1)}, s32[]{:T(128)}, ...), condition=%wide.region_6.7_spmd, body=%wide.region_5.6_spmd.sunk | while | flops 262150 | bytes 1310863 | solution.py:35
  324.4 1.2 convert_add_fusion.5
  332.6 3.5 fusion.7
  336.1 2.3 fusion.9
  338.7 1.6 copy-done.12
  340.4 19.9 %convolution_convert_fusion = bf16[512,4096]{1,0:T(8,128)(2,1)} fusion(bf16[512,3072]{0,1:T(8,128)(2,1)S(1)} %bitcast.162, bf16[4096,3072]{0,1:T(8,128)(2,1)} %bitcast.149), kind=kOutput, calls=%fused_computation.11 | convolution fusion | flops 12886999040 | bytes 32505856 | tf_op jit(solution)/shard_map/tc,mc->tm/dot_general | solution.py:133
  360.3 8.0 %broadcast_in_dim.58 = f32[32,128,8,128]{1,0,3,2:T(8,128)} broadcast(f32[32,8]{0,1:T(8,128)S(1)} %get-tuple-element.113), dimensions={0,2} | broadcast | bytes 16778240 | tf_op jit(solution)/shard_map/broadcast_in_dim | solution.py:40
  368.3 15.5 %fusion.1 = bf16[4096,1024]{0,1:T(8,128)(2,1)} fusion(f32[128,8,32,128]{3,2,1,0:T(8,128)} %bitcast.143, bf16[512,1024]{0,1:T(8,128)(2,1)S(1)} %bitcast.161, bf16[512,4096]{1,0:T(8,128)(2,1)S(1)} %copy-done.6), kind=kOutput, calls=%fused_computation.6 | convolution fusion | flops 4303355904 | bytes 30408704 | tf_op jit(solution)/shard_map/tm,tf->mf/dot_general | solution.py:146
  383.8 27.2 %fusion = bf16[4096,3072]{0,1:T(8,128)(2,1)} fusion(bf16[4096,3072]{0,1:T(8,128)(2,1)} %bitcast.144, bf16[512,3072]{0,1:T(8,128)(2,1)} %bitcast.163, bf16[512,4096]{1,0:T(8,128)(2,1)} %all-gather.7.cloned.1.call-done), kind=kOutput, calls=%fused_computation.3 | convolution fusion | flops 12922650624 | bytes 57671680 | tf_op jit(solution)/shard_map/tm,tc->mc/dot_general | solution.py:144
  411.0 24.0 %pad_maximum_fusion = bf16[4096,4096]{0,1:T(8,128)(2,1)} fusion(bf16[4096,1024]{0,1:T(8,128)(2,1)} %fusion.1, bf16[4096,3072]{0,1:T(8,128)(2,1)} %fusion), kind=kLoop, calls=%fused_computation.4 | loop fusion | flops 67108864 | bytes 67108864 | tf_op jit(solution)/shard_map/concatenate | solution.py:149
  435.1 1.1 copy-done.9
  436.2 2.4 add_convert_fusion.2
  438.7 44.7 %reduce-scatter.6.cloned.1.call-done = bf16[128,4096]{1,0:T(8,128)(2,1)} async-done(((bf16[512,4096]{1,0:T(8,128)(2,1)}), bf16[128,4096]{1,0:T(8,128)(2,1)}) %reduce-scatter.6.cloned.1.call-update) | async-done | bytes 1048592 | tf_op jit(solution)/shard_map/reduce_scatter | solution.py:132
  483.4 2.4 add_convert_fusion
  485.8 206.9 %reduce-scatter.8.cloned.1.call-done = bf16[512,4096]{0,1:T(8,128)(2,1)} async-done(((bf16[4096,4096]{0,1:T(8,128)(2,1)}), bf16[512,4096]{0,1:T(8,128)(2,1)}) %reduce-scatter.8.cloned.1.call-update) | async-done | bytes 4194320 | tf_op jit(solution)/shard_map/reduce_scatter | solution.py:148
  692.7 3.4 convert_multiply_fusion.1
  696.1 3.3 slice.41
  699.4 1.5 slice_bitcast_fusion
  700.9 6.6 copy.56
  (65 shorter events, 10.7 us)
Async XLA Ops:
  7.2 138.5 %all-gather.7.cloned.1.call-start = ((), (), s32[]{:S(2)}) async-start(), calls=%async_computation.3 | async-start | bytes 5242880 | tf_op jit(solution)/shard_map/all_gather | solution.py:67
  7.9 32.3 %copy-start.15 = (s32[3,32,8]{1,2,0:T(8,128)S(1)}, s32[3,32,8]{1,2,0:T(8,128)}, u32[]{:S(2)}) copy-start(s32[3,32,8]{1,2,0:T(8,128)} %param.16) | copy-start | bytes 9220
  7.9 187.5 %all-gather.11.cloned.1.call-start = ((), (), s32[]{:S(2)}) async-start(), calls=%async_computation.8 | async-start | bytes 2359296 | tf_op jit(solution)/shard_map/all_gather | solution.py:13
  117.0 28.6 %copy-start.13 = (s32[512,8]{0,1:T(8,128)S(1)}, s32[512,8]{0,1:T(8,128)}, u32[]{:S(2)}) copy-start(s32[512,8]{0,1:T(8,128)} %param.13) | copy-start | bytes 49156
  117.0 28.6 %copy-start.14 = (s32[512,8]{0,1:T(8,128)S(1)}, s32[512,8]{0,1:T(8,128)}, u32[]{:S(2)}) copy-start(s32[512,8]{0,1:T(8,128)} %param.14) | copy-start | bytes 49156
  163.8 4.0 copy-start.1
  163.8 2.6 copy-start.16
  165.4 112.4 %all-gather.9.cloned.1.call-start = ((), (), s32[]{:S(2)}) async-start(), calls=%async_computation.5 | async-start | bytes 5242880 | tf_op jit(solution)/shard_map/all_gather | solution.py:99
  166.1 158.2 %all-gather.13.cloned.1.call-start = ((), (), s32[]{:S(2)}) async-start(), calls=%async_computation.9 | async-start | bytes 2359296 | tf_op jit(solution)/shard_map/all_gather | solution.py:26
  167.9 2.0 copy-start.4
  198.6 80.4 %copy-start.3 = (f32[8,128,512]{2,1,0:T(8,128)}, f32[8,128,512]{2,1,0:T(8,128)S(1)}, u32[]{:S(2)}) copy-start(f32[8,128,512]{2,1,0:T(8,128)S(1)} %get-tuple-element.125) | copy-start | bytes 6291460
  279.0 12.4 %copy-start = (bf16[8,128,32,128]{3,2,1,0:T(8,128)(2,1)}, bf16[8,128,32,128]{3,2,1,0:T(8,128)(2,1)S(1)}, u32[]{:S(2)}) copy-start(bf16[8,128,32,128]{3,2,1,0:T(8,128)(2,1)S(1)} %broadcast_in_dim.30) | copy-start | bytes 25165828
  297.7 137.3 %reduce-scatter.4.cloned.1.call-start = ((), (), s32[]{:S(2)}) async-start(), calls=%async_computation.4 | async-start | bytes 5242880 | tf_op jit(solution)/shard_map/reduce_scatter | solution.py:92
  311.5 171.9 %reduce-scatter.6.cloned.1.call-start = ((), (), s32[]{:S(2)}) async-start(), calls=%async_computation.6 | async-start | bytes 5242880 | tf_op jit(solution)/shard_map/reduce_scatter | solution.py:132
  311.5 2.7 copy-start.2
  318.6 3.0 copy-start.5
  324.3 11.8 %copy-start.7 = (f32[8,128,512]{2,1,0:T(8,128)S(1)}, f32[8,128,512]{2,1,0:T(8,128)}, u32[]{:S(2)}) copy-start(f32[8,128,512]{2,1,0:T(8,128)} %fusion.17) | copy-start | bytes 6291460
  332.5 5.8 copy-start.11
  338.7 1.6 copy-start.12
  360.3 332.4 %reduce-scatter.8.cloned.1.call-start = ((), (), s32[]{:S(2)}) async-start(), calls=%async_computation.7 | async-start | bytes 37748736 | tf_op jit(solution)/shard_map/reduce_scatter | solution.py:148
  360.3 8.0 %copy-start.6 = (bf16[512,4096]{1,0:T(8,128)(2,1)S(1)}, bf16[512,4096]{1,0:T(8,128)(2,1)}, u32[]{:S(2)}) copy-start(bf16[512,4096]{1,0:T(8,128)(2,1)} %all-gather.9.cloned.1.call-done) | copy-start | bytes 12582916
  360.3 8.0 %copy-start.8 = (bf16[512,8,128]{0,2,1:T(8,128)(2,1)S(1)}, bf16[512,8,128]{0,2,1:T(8,128)(2,1)}, u32[]{:S(2)}) copy-start(bf16[512,8,128]{0,2,1:T(8,128)(2,1)} %get-tuple-element.120) | copy-start | bytes 3145732
  435.0 1.2 copy-start.9
  435.0 48.4 %copy-start.10 = (bf16[128,4096]{1,0:T(8,128)(2,1)S(1)}, bf16[128,4096]{1,0:T(8,128)(2,1)}, u32[]{:S(2)}) copy-start(bf16[128,4096]{1,0:T(8,128)(2,1)} %param.19) | copy-start | bytes 3145732
Sparse Core Ops, SparseCore 0:
  9.6 83.4 all-gather.6
  165.5 29.8 all-gather.10
  197.0 80.7 all-gather.8
  297.8 26.4 all-gather.12
  327.0 76.7 reduce-scatter.3
  406.1 77.2 reduce-scatter.5
  486.9 205.7 reduce-scatter.7
where the time goes:
time: 725 us; the launch traced here: 715 us
  waiting for transfers between devices  356 us (49%)
  matrix products  136 us (19%)
  local copies, waits for them, and re-layouts  135 us (19%)
  other arithmetic  72 us (10%)
  between operations  14.7 us (2%)
    reduce_scatter x1, waiting for transfers between devices, on_device(): lax.psum_scatter(jnp.concatenate([qkv_part, out_part], axis=1).astype(jnp...  207 us
    all_gather x1, waiting for transfers between devices, on_device(): grad_rows = lax.all_gather(cotangent, 'tp', axis=0, tiled=True)  79.2 us
    unnamed x38, local copies, waits for them, and re-layouts  60 us
    another operation x4, local copies, waits for them, and re-layouts, qkv_keep_table(): return jnp.stack(tables, axis=1)  47.8 us
    reduce_scatter x1, waiting for transfers between devices, on_device(): lax.psum_scatter(jnp.einsum('tc,mc->tm', row_piece, qkv_used, preferred_e...  44.7 us
    mul x1, other arithmetic, on_device(): qkv_used = qkv_weight.reshape(model_width, 3 * features) * qkv_keep  28.6 us
    dot_general x1, matrix products, on_device(): jnp.einsum('tm,tc->mc', gathered, grad_proj, preferred_element_type=jnp.f...  27.2 us
    concatenate x1, other arithmetic, on_device(): jnp.concatenate([qkv_part, out_part], axis=1).astype(jnp.bfloat16)  24 us
  transfers between devices with their start and end apart: 7, of which 5 were waited for; matrix products, arithmetic and copies ran while one was open for 40% of the time, Pallas kernels for 0%

commit v1 on v0

--- a/solution.py
+++ b/solution.py
@@ -1,3 +1,4 @@
+import functools
 import math
 import jax
 import jax.numpy as jnp
@@ -6,6 +7,22 @@
 
 BLOCK = 128
 EPSILON = 1e-05
+
+
+def update_the_windows(local_x, mesh_dim, along_dim):
+    sides = lax.psum(1, mesh_dim)
+    store = [local_x]
+    for j0 in range(sides - 1):
+        carry = lax.ppermute(
+            store[-1], mesh_dim, [(dev, (dev + 1) % sides) for dev in range(sides)]
+        )
+        store.append(carry)
+    q_next = jnp.concatenate(store[::-1], along_dim)
+    z2 = lax.axis_index(mesh_dim)
+    return jnp.roll(q_next, (z2 + 1) * local_x.shape[along_dim], axis=along_dim)
+
+
+time_frame_on = functools.partial(update_the_windows, mesh_dim="tp", along_dim=0)
 
 
 def carried_in(value, axis, join, neutral):
@@ -96,7 +113,7 @@
         tiled=True,
     ).astype(jnp.float32)
     layer_out = (tokens.astype(jnp.float32) + head_sum).astype(jnp.bfloat16)
-    grad_rows = lax.all_gather(cotangent, "tp", axis=0, tiled=True)
+    grad_rows = time_frame_on(cotangent)
     grad_attended = jnp.einsum("tm,fm->tf", grad_rows, out_used, preferred_element_type=jnp.float32)
     grad_attended = grad_attended.reshape(block_rows, local_heads, head_width)
     inner_mean = jnp.mean(grad_attended * normed, axis=-1, keepdims=True)

time: 725 us -> 676 us (0.932)
  waiting for transfers between devices: 356 us -> 285 us
  local copies, waits for them, and re-layouts: 135 us -> 146 us
  matrix products: 136 us -> 144 us
    all_gather x1 -> x0, waiting for transfers between devices: 79.2 us -> none  [on_device(): grad_rows = lax.all_gather(cotangent, 'tp', axis=0, tiled=True)]
    ppermute x0 -> x3, waiting for transfers between devices: none -> 12.2 us  [update_the_windows(): lax.ppermute(store[-1], mesh_dim, [(dev, (dev + 1) % sides) for dev in ra...]
    unnamed x38 -> x53, local copies, waits for them, and re-layouts: 60 us -> 70.1 us
    all_gather x1, waiting for transfers between devices: 22.8 us -> 12.9 us  [carried_in(): gathered = lax.all_gather(value.astype(jnp.bfloat16), axis)]
    all_gather x1, waiting for transfers between devices: 0.59 us -> 9.61 us  [entering(): lax.all_gather(value.astype(jnp.bfloat16 if value.dtype == jnp.float32 el...]
  transfers between devices with their start and end apart: 7 -> 9, of which waited for: 5 -> 5; matrix products, arithmetic and copies ran while one was open for 40% -> 44% of each run, Pallas kernels for 0% -> 0%
where the time goes in v1:
time: 676 us; the launch traced here: 668 us
  waiting for transfers between devices  285 us (42%)
  local copies, waits for them, and re-layouts  146 us (22%)
  matrix products  144 us (21%)
  other arithmetic  72.3 us (11%)
  between operations  14.7 us (2%)
    reduce_scatter x1, waiting for transfers between devices, on_device(): lax.psum_scatter(jnp.concatenate([qkv_part, out_part], axis=1).astype(jnp...  207 us
    unnamed x53, local copies, waits for them, and re-layouts  70.1 us
    another operation x4, local copies, waits for them, and re-layouts, qkv_keep_table(): return jnp.stack(tables, axis=1)  48 us
    reduce_scatter x1, waiting for transfers between devices, on_device(): lax.psum_scatter(jnp.einsum('tc,mc->tm', row_piece, qkv_used, preferred_e...  42.7 us
    mul x1, other arithmetic, on_device(): qkv_used = qkv_weight.reshape(model_width, 3 * features) * qkv_keep  28.6 us
    dot_general x1, matrix products, on_device(): jnp.einsum('tm,tc->mc', gathered, grad_proj, preferred_element_type=jnp.f...  25.9 us
    concatenate x1, other arithmetic, on_device(): jnp.concatenate([qkv_part, out_part], axis=1).astype(jnp.bfloat16)  23.5 us
    broadcast_in_dim x5, local copies, waits for them, and re-layouts, expand_blocks(): jnp.broadcast_to(blocks.astype(jnp.bfloat16)[:, None, :, None], (row_bloc...  22.3 us
  transfers between devices with their start and end apart: 9, of which 5 were waited for; matrix products, arithmetic and copies ran while one was open for 44% of the time, Pallas kernels for 0%

profile of v1, /device:TPU:0, one launch (start us, length us, event | category | flops | bytes accessed | tf_op | source)
XLA Modules:
  0.0 668.4 jit_solution(1887015115992455011)
XLA Ops:
  7.9 3.1 collective-permute-start
  11.0 33.6 %copy.45 = bf16[4096,3,1024]{0,2,1:T(8,128)(2,1)} copy(bf16[4096,3,1024]{2,0,1:T(8,128)(2,1)} %param.15) | data formatting | bytes 50331648 | tf_op args[3]
  44.7 4.4 broadcast_in_dim.22
  49.1 13.3 %stack_reshape.9 = bf16[4096,1,1024]{0,2,1:T(8,128)(2,1)} reshape(bf16[32,128,8,128]{1,0,3,2:T(8,128)(2,1)} %broadcast_in_dim.22) | data formatting | bytes 16777216 | tf_op jit(solution)/shard_map/stack;reshape | solution.py:65
  62.4 4.4 broadcast_in_dim.25
  66.8 13.3 %stack_reshape.10 = bf16[4096,1,1024]{0,2,1:T(8,128)(2,1)} reshape(bf16[32,128,8,128]{1,0,3,2:T(8,128)(2,1)} %broadcast_in_dim.25) | data formatting | bytes 16777216 | tf_op jit(solution)/shard_map/stack;reshape | solution.py:65
  80.1 4.4 broadcast_in_dim.26
  84.5 13.3 %stack_reshape.11 = bf16[4096,1,1024]{0,2,1:T(8,128)(2,1)} reshape(bf16[32,128,8,128]{1,0,3,2:T(8,128)(2,1)} %broadcast_in_dim.26) | data formatting | bytes 16777216 | tf_op jit(solution)/shard_map/stack;reshape | solution.py:65
  99.1 7.7 %constant_dynamic-update-slice_fusion.2 = bf16[4096,3,1024]{0,2,1:T(8,128)(2,1)} fusion(bf16[4096,1,1024]{0,2,1:T(8,128)(2,1)} %stack_reshape.9), kind=kLoop, calls=%fused_computation.52 | loop fusion | bytes 16777216
  106.8 7.8 %constant_dynamic-update-slice_fusion.1 = bf16[4096,3,1024]{0,2,1:T(8,128)(2,1)} fusion(bf16[4096,3,1024]{0,2,1:T(8,128)(2,1)} %constant_dynamic-update-slice_fusion.2, bf16[4096,1,1024]{0,2,1:T(8,128)(2,1)} %stack_reshape.10), kind=kLoop, calls=%fused_computation.51 | loop fusion | bytes 16777216
  114.6 12.2 %collective-permute-done.1 = bf16[128,4096]{1,0:T(8,128)(2,1)S(1)} collective-permute-done((bf16[128,4096]{1,0:T(8,128)(2,1)S(1)}, bf16[128,4096]{1,0:T(8,128)(2,1)S(1)}, u32[]{:S(2)}, u32[]{:S(2)}) %collective-permute-start.1) | collective-permute-done | bytes 1048608 | tf_op jit(solution)/shard_map/ppermute | solution.py:16
  126.9 8.0 %constant_dynamic-update-slice_fusion = bf16[4096,3,1024]{0,2,1:T(8,128)(2,1)} fusion(bf16[4096,3,1024]{0,2,1:T(8,128)(2,1)} %constant_dynamic-update-slice_fusion.1, bf16[4096,1,1024]{0,2,1:T(8,128)(2,1)} %stack_reshape.11), kind=kLoop, calls=%fused_computation.50 | loop fusion | bytes 16777216 | tf_op jit(solution)/shard_map/stack | solution.py:65
  135.0 28.6 %mul.85 = bf16[4096,3,1024]{0,2,1:T(8,128)(2,1)} multiply(bf16[4096,3,1024]{0,2,1:T(8,128)(2,1)} %copy.45, bf16[4096,3,1024]{0,2,1:T(8,128)(2,1)} %constant_dynamic-update-slice_fusion) | non-fusion elementwise | flops 12582912 | bytes 75497472 | tf_op jit(solution)/shard_map/mul | solution.py:82
  165.1 18.2 %convolution_convert_fusion.2 = bf16[3072,512]{1,0:T(8,128)(2,1)S(1)} fusion(bf16[4096,3072]{0,1:T(8,128)(2,1)} %bitcast.142, bf16[512,4096]{1,0:T(8,128)(2,1)} %all-gather.6.cloned.1.call-done), kind=kOutput, calls=%fused_computation.13 | convolution fusion | flops 12886474752 | bytes 32505856 | tf_op jit(solution)/shard_map/dot_general | solution.py:85
  183.3 1.5 convolution_convert_fusion.3
  184.9 2.5 constant_dynamic-update-slice_fusion.9
  187.3 2.4 constant_dynamic-update-slice_fusion.8
  195.0 1.4 select_convert_fusion.1
  196.5 2.0 copy-done.3
  198.4 2.8 fusion.14
  201.2 12.9 %all-gather.8.cloned.1.call-done = bf16[64,128,128]{2,1,0:T(8,128)(2,1)} async-done(((bf16[8,128,128]{2,1,0:T(8,128)(2,1)}), bf16[64,128,128]{2,1,0:T(8,128)(2,1)}) %all-gather.8.cloned.1.call-update) | async-done | bytes 2097168 | tf_op jit(solution)/shard_map/all_gather | solution.py:30
  214.3 4.4 fusion.7
  219.9 15.7 %multiply_reduce_fusion = (f32[512,8]{0,1:T(8,128)S(1)}, f32[512,1024]{0,1:T(8,128)}) fusion(f32[8,128,512]{2,1,0:T(8,128)} %get-tuple-element.125, f32[512,8]{0,1:T(8,128)S(1)} %add_rsqrt_fusion, bf16[1024,4096]{1,0:T(8,128)(2,1)} %param.17, bf16[128,8,32,128]{3,2,1,0:T(8,128)(2,1)S(1)} %bitcast.139, ...), kind=kOutput, calls=%fused_computation.29 | convolution fusion | flops 4300730368 | bytes 25198596 | tf_op jit(solution)/shard_map/tm,fm->tf/dot_general | solution.py:117
  235.6 3.9 subtract_multiply_fusion
  239.5 3.1 convolution_convert_fusion.4
  243.1 13.3 %convolution_convert_fusion.1 = bf16[512,4096]{1,0:T(8,128)(2,1)} fusion(bf16[512,1024]{0,1:T(8,128)(2,1)} %bitcast.154, bf16[1024,4096]{1,0:T(8,128)(2,1)} %param.17, bf16[128,8,32,128]{3,2,1,0:T(8,128)(2,1)} %bitcast.140), kind=kOutput, calls=%fused_computation.12 | convolution fusion | flops 4301258752 | bytes 22020096 | tf_op jit(solution)/shard_map/dot_general | solution.py:110
  256.5 2.8 select_convert_fusion
  259.3 1.5 fusion.24
  260.7 2.9 fusion.10
  263.6 2.1 fusion.19
  266.6 2.0 fusion.15
  268.6 9.6 %all-gather.10.cloned.1.call-done = bf16[64,128,128]{2,1,0:T(8,128)(2,1)} async-done(((bf16[8,128,128]{2,1,0:T(8,128)(2,1)}), bf16[64,128,128]{2,1,0:T(8,128)(2,1)}) %all-gather.10.cloned.1.call-update) | async-done | bytes 2097168 | tf_op jit(solution)/shard_map/all_gather | solution.py:43
  278.3 8.0 %while.23 = (s32[]{:T(128)}, f32[8,128,128]{2,1,0:T(8,128)S(1)}, s32[]{:T(128)}, bf16[8,8,128,128]{3,2,1,0:T(8,128)(2,1)}, s32[]{:T(128)}, /*index=5*/s32[]{:T(128)}, s32[]{:T(128)}, s32[]{:T(128)}) while((s32[]{:T(128)}, f32[8,128,128]{2,1,0:T(8,128)S(1)}, s32[]{:T(128)}, bf16[8,8,128,128]{3,2,1,0:T(8,128)(2,1)}, s32[]{:T(128)}, ...), condition=%wide.region_6.7_spmd, body=%wide.region_5.6_spmd.sunk | while | flops 262150 | bytes 1310863 | solution.py:52
  286.2 3.6 fusion.9
  289.9 2.3 fusion.11
  292.5 19.6 %convolution_convert_fusion = bf16[512,4096]{1,0:T(8,128)(2,1)} fusion(bf16[512,3072]{0,1:T(8,128)(2,1)S(1)} %bitcast.156, bf16[4096,3072]{0,1:T(8,128)(2,1)} %bitcast.143), kind=kOutput, calls=%fused_computation.11 | convolution fusion | flops 12886999040 | bytes 32505856 | tf_op jit(solution)/shard_map/tc,mc->tm/dot_general | solution.py:150
  312.4 8.0 %broadcast_in_dim.58 = f32[32,128,8,128]{1,0,3,2:T(8,128)} broadcast(f32[32,8]{0,1:T(8,128)S(1)} %get-tuple-element.113), dimensions={0,2} | broadcast | bytes 16778240 | tf_op jit(solution)/shard_map/broadcast_in_dim | solution.py:57
  320.4 21.1 %fusion.1 = bf16[4096,1024]{0,1:T(8,128)(2,1)} fusion(f32[128,8,32,128]{3,2,1,0:T(8,128)} %bitcast.137, bf16[512,1024]{0,1:T(8,128)(2,1)S(1)} %bitcast.155, bf16[1024,4096]{1,0:T(8,128)(2,1)} %constant_dynamic-update-slice_fusion.3, s32[]{:T(128)S(6)} %select_n.33), kind=kOutput, calls=%fused_computation.6 | convolution fusion | flops 4303355904 | bytes 30408708 | tf_op jit(solution)/shard_map/tm,tf->mf/dot_general | solution.py:163
  341.5 25.9 %fusion = bf16[4096,3072]{0,1:T(8,128)(2,1)} fusion(bf16[4096,3072]{0,1:T(8,128)(2,1)} %bitcast.138, bf16[512,3072]{0,1:T(8,128)(2,1)S(1)} %bitcast.157, bf16[512,4096]{1,0:T(8,128)(2,1)} %all-gather.6.cloned.1.call-done), kind=kOutput, calls=%fused_computation.3 | convolution fusion | flops 12922650624 | bytes 57671680 | tf_op jit(solution)/shard_map/tm,tc->mc/dot_general | solution.py:161
  367.4 23.5 %pad_maximum_fusion = bf16[4096,4096]{0,1:T(8,128)(2,1)} fusion(bf16[4096,1024]{0,1:T(8,128)(2,1)} %fusion.1, bf16[4096,3072]{0,1:T(8,128)(2,1)} %fusion), kind=kLoop, calls=%fused_computation.4 | loop fusion | flops 67108864 | bytes 67108864 | tf_op jit(solution)/shard_map/concatenate | solution.py:166
  392.1 2.4 add_convert_fusion.2
  394.6 42.7 %reduce-scatter.6.cloned.1.call-done = bf16[128,4096]{1,0:T(8,128)(2,1)} async-done(((bf16[512,4096]{1,0:T(8,128)(2,1)}), bf16[128,4096]{1,0:T(8,128)(2,1)}) %reduce-scatter.6.cloned.1.call-update) | async-done | bytes 1048592 | tf_op jit(solution)/shard_map/reduce_scatter | solution.py:149
  437.3 2.4 add_convert_fusion
  439.7 206.8 %reduce-scatter.8.cloned.1.call-done = bf16[512,4096]{0,1:T(8,128)(2,1)} async-done(((bf16[4096,4096]{0,1:T(8,128)(2,1)}), bf16[512,4096]{0,1:T(8,128)(2,1)}) %reduce-scatter.8.cloned.1.call-update) | async-done | bytes 4194320 | tf_op jit(solution)/shard_map/reduce_scatter | solution.py:165
  646.5 3.4 convert_multiply_fusion.1
  649.9 3.3 slice.41
  653.2 1.5 slice_bitcast_fusion
  654.7 6.6 copy.59
  (84 shorter events, 21.4 us)
Async XLA Ops:
  7.2 157.8 %all-gather.6.cloned.1.call-start = ((), (), s32[]{:S(2)}) async-start(), calls=%async_computation.3 | async-start | bytes 5242880 | tf_op jit(solution)/shard_map/all_gather | solution.py:84
  7.9 206.2 %all-gather.8.cloned.1.call-start = ((), (), s32[]{:S(2)}) async-start(), calls=%async_computation.7 | async-start | bytes 2359296 | tf_op jit(solution)/shard_map/all_gather | solution.py:30
  7.9 89.8 %collective-permute-start = (bf16[128,4096]{1,0:T(8,128)(2,1)}, bf16[128,4096]{1,0:T(8,128)(2,1)S(1)}, u32[]{:S(2)}, u32[]{:S(2)}) collective-permute-start(bf16[128,4096]{1,0:T(8,128)(2,1)} %param.19), channel_id=1, source_target_pairs={{0,1},{1,2},{2,3},{3,0},{4,5},{5,6},{6,7},{7,4},{8,9},{9,10},{10,1... | collective-permute-start | bytes 3145736 | tf_op jit(solution)/shard_map/ppermute | solution.py:16
  11.0 33.6 %copy-start.19 = (s32[3,32,8]{1,2,0:T(8,128)S(1)}, s32[3,32,8]{1,2,0:T(8,128)}, u32[]{:S(2)}) copy-start(s32[3,32,8]{1,2,0:T(8,128)} %param.16) | copy-start | bytes 9220
  97.8 9.1 %copy-start.10 = (bf16[128,4096]{1,0:T(8,128)(2,1)}, bf16[128,4096]{1,0:T(8,128)(2,1)S(1)}, u32[]{:S(2)}) copy-start(bf16[128,4096]{1,0:T(8,128)(2,1)S(1)} %collective-permute-done) | copy-start | bytes 3145732
  97.8 29.0 %collective-permute-start.1 = (bf16[128,4096]{1,0:T(8,128)(2,1)S(1)}, bf16[128,4096]{1,0:T(8,128)(2,1)S(1)}, u32[]{:S(2)}, u32[]{:S(2)}) collective-permute-start(bf16[128,4096]{1,0:T(8,128)(2,1)S(1)} %collective-permute-done), channel_id=1, source_target_pairs={{0,1},{1,2},{2,3},{3,0},{4,5},{5,6},{6,7},{7,4},{8,9},{9,10},{10,1... | collective-permute-start | bytes 3145736 | tf_op jit(solution)/shard_map/ppermute | solution.py:16
  126.8 8.2 %copy-start.12 = (bf16[128,4096]{1,0:T(8,128)(2,1)}, bf16[128,4096]{1,0:T(8,128)(2,1)S(1)}, u32[]{:S(2)}) copy-start(bf16[128,4096]{1,0:T(8,128)(2,1)S(1)} %collective-permute-done.1) | copy-start | bytes 3145732
  126.8 37.0 %collective-permute-start.2 = (bf16[128,4096]{1,0:T(8,128)(2,1)S(1)}, bf16[128,4096]{1,0:T(8,128)(2,1)S(1)}, u32[]{:S(2)}, u32[]{:S(2)}) collective-permute-start(bf16[128,4096]{1,0:T(8,128)(2,1)S(1)} %collective-permute-done.1), channel_id=1, source_target_pairs={{0,1},{1,2},{2,3},{3,0},{4,5},{5,6},{6,7},{7,4},{8,9},{9,10},{10,1... | collective-permute-start | bytes 3145736 | tf_op jit(solution)/shard_map/ppermute | solution.py:16
  135.0 28.7 %copy-start.20 = (s32[8,32]{1,0:T(8,128)S(1)}, s32[8,32]{1,0:T(8,128)}, u32[]{:S(2)}) copy-start(s32[8,32]{1,0:T(8,128)} %param.18) | copy-start | bytes 3076
  135.0 28.7 %copy-start.17 = (s32[512,8]{0,1:T(8,128)S(1)}, s32[512,8]{0,1:T(8,128)}, u32[]{:S(2)}) copy-start(s32[512,8]{0,1:T(8,128)} %param.13) | copy-start | bytes 49156
  135.0 28.7 %copy-start.18 = (s32[512,8]{0,1:T(8,128)S(1)}, s32[512,8]{0,1:T(8,128)}, u32[]{:S(2)}) copy-start(s32[512,8]{0,1:T(8,128)} %param.14) | copy-start | bytes 49156
  163.8 1.3 copy-start.14
  183.3 13.2 %copy-start.1 = (bf16[3072,512]{1,0:T(8,128)(2,1)}, bf16[3072,512]{1,0:T(8,128)(2,1)S(1)}, u32[]{:S(2)}) copy-start(bf16[3072,512]{1,0:T(8,128)(2,1)S(1)} %convolution_convert_fusion.2) | copy-start | bytes 9437188
  184.8 93.4 %all-gather.10.cloned.1.call-start = ((), (), s32[]{:S(2)}) async-start(), calls=%async_computation.8 | async-start | bytes 2359296 | tf_op jit(solution)/shard_map/all_gather | solution.py:43
  184.8 4.9 copy-start.5
  184.8 6.0 copy-start.15
  184.8 7.0 %copy-start.13 = (bf16[128,4096]{1,0:T(8,128)(2,1)S(1)}, bf16[128,4096]{1,0:T(8,128)(2,1)}, u32[]{:S(2)}) copy-start(bf16[128,4096]{1,0:T(8,128)(2,1)} %copy-done.12) | copy-start | bytes 3145732
  187.3 5.6 copy-start.11
  196.5 2.0 copy-start.3
  219.9 15.7 %copy-start = (bf16[8,128,32,128]{3,2,1,0:T(8,128)(2,1)}, bf16[8,128,32,128]{3,2,1,0:T(8,128)(2,1)S(1)}, u32[]{:S(2)}) copy-start(bf16[8,128,32,128]{3,2,1,0:T(8,128)(2,1)S(1)} %broadcast_in_dim.30) | copy-start | bytes 25165828
  242.6 148.4 %reduce-scatter.4.cloned.1.call-start = ((), (), s32[]{:S(2)}) async-start(), calls=%async_computation.4 | async-start | bytes 5242880 | tf_op jit(solution)/shard_map/reduce_scatter | solution.py:109
  256.4 180.9 %reduce-scatter.6.cloned.1.call-start = ((), (), s32[]{:S(2)}) async-start(), calls=%async_computation.5 | async-start | bytes 5242880 | tf_op jit(solution)/shard_map/reduce_scatter | solution.py:149
  256.5 2.8 copy-start.2
  263.6 2.9 copy-start.4
  278.3 11.6 %copy-start.7 = (f32[8,128,512]{2,1,0:T(8,128)S(1)}, f32[8,128,512]{2,1,0:T(8,128)}, u32[]{:S(2)}) copy-start(f32[8,128,512]{2,1,0:T(8,128)} %fusion.19) | copy-start | bytes 6291460
  286.2 5.9 copy-start.16
  312.1 334.3 %reduce-scatter.8.cloned.1.call-start = ((), (), s32[]{:S(2)}) async-start(), calls=%async_computation.6 | async-start | bytes 37748736 | tf_op jit(solution)/shard_map/reduce_scatter | solution.py:165
  312.4 8.0 %copy-start.8 = (bf16[512,8,128]{0,2,1:T(8,128)(2,1)S(1)}, bf16[512,8,128]{0,2,1:T(8,128)(2,1)}, u32[]{:S(2)}) copy-start(bf16[512,8,128]{0,2,1:T(8,128)(2,1)} %get-tuple-element.120) | copy-start | bytes 3145732
  390.9 1.2 copy-start.9
  390.9 46.4 %copy-start.6 = (bf16[128,4096]{1,0:T(8,128)(2,1)S(1)}, bf16[128,4096]{1,0:T(8,128)(2,1)}, u32[]{:S(2)}) copy-start(bf16[128,4096]{1,0:T(8,128)(2,1)} %param.19) | copy-start | bytes 3145732
Sparse Core Ops, SparseCore 0:
  9.6 97.1 all-gather.5
  184.9 29.1 all-gather.7
  242.7 35.4 all-gather.9
  280.9 76.7 reduce-scatter.3
  360.0 77.2 reduce-scatter.5
  440.7 205.7 reduce-scatter.7
